TPU v7x, 32 devices: a whole 2x2x4 slice. The times are simulated.
32 devices in a mesh: depth: 4 (over y, x), lat: 8 (over z, core).
Axes of the slice: x: 2, y: 2, z: 4, core: 2. Of those that a mesh axis runs over, the one named last changes fastest.
Arguments:
- sources: bfloat16 [4, 8, 32, 2048], P('depth', 'lat'), may hold values from -6 to 6
- coupling: float32 [4, 8, 2048], P('depth', 'lat'), may hold values from 0.2 to 0.6
- merge_ops: bfloat16 [4, 8, 2048, 2048], P('depth', 'lat'), may hold values from -1 to 1.5
Outputs:
- solution: bfloat16 [4, 8, 32, 2048], P('depth', 'lat')
All inputs are finite; a program needn't handle non-finite values.
Results may differ from a plain program's by a relative error of at most 0.03.
Values may be sent and summed in bfloat16 or wider, within the bound.
No kernel may reach another device: no remote copies, remote signals or barrier semaphores. Data moves between devices by JAX's collectives and lax.ppermute only.
A program may use at most 64 MiB of HBM per device.

v0:
```python
import functools

import jax
import jax.numpy as jnp
from jax import lax
from jax.experimental import pallas as pl
from jax.experimental.pallas import tpu as pltpu
from jax.sharding import PartitionSpec as P


half_root = 0.7071067811865476
TILE = 512


def partner_2(block, axis, apart):
    count = lax.axis_size(axis)
    route = []
    for low in range(count):
        high = low | 1 << apart
        if high != low and high < count:
            route += [(low, high), (high, low)]
    return lax.ppermute(block, axis, route)


def handed_down(array, axis, layer):
    return lax.ppermute(array, axis, [(layer, layer + 1)])


def mixed_dot_kernel(sign_ref, values_ref, partner_ref, op_ref, out_ref):
    first = values_ref[...].astype(jnp.float32)
    second = partner_ref[...].astype(jnp.float32)
    mixed = ((second + sign_ref[...] * first) * half_root).astype(jnp.bfloat16)
    width = op_ref.shape[1]
    for start in range(0, width, TILE):
        out_ref[:, start:start + TILE] = jnp.dot(
            mixed, op_ref[:, start:start + TILE], preferred_element_type=jnp.float32
        ).astype(out_ref.dtype)


def transposed_dot_kernel(values_ref, op_ref, out_ref):
    values = values_ref[...]
    width = op_ref.shape[0]
    for start in range(0, width, TILE):
        block = lax.dot_general(
            op_ref[start:start + TILE, :],
            values,
            (((1,), (1,)), ((), ())),
            preferred_element_type=jnp.float32,
        )
        out_ref[:, start:start + TILE] = block.T.astype(out_ref.dtype)


def vmem_spec():
    return pl.BlockSpec(memory_space=pltpu.VMEM)


def cost(rows, width):
    return pl.CostEstimate(
        flops=2 * rows * width * width,
        bytes_accessed=2 * width * width + 6 * rows * width,
        transcendentals=0,
    )


def mixed_dot(sign, values, partner, merge_op):
    rows, width = values.shape
    return pl.pallas_call(
        mixed_dot_kernel,
        out_shape=jax.ShapeDtypeStruct(values.shape, jnp.bfloat16),
        in_specs=[vmem_spec()] * 4,
        out_specs=vmem_spec(),
        cost_estimate=cost(rows, width),
        compiler_params=pltpu.CompilerParams(vmem_limit_bytes=4 * 1024 * 1024),
    )(sign, values, partner, pltpu.with_memory_space_constraint(merge_op, pltpu.VMEM))


def transposed_dot(values, merge_op):
    rows, width = values.shape
    return pl.pallas_call(
        transposed_dot_kernel,
        out_shape=jax.ShapeDtypeStruct(values.shape, jnp.bfloat16),
        in_specs=[vmem_spec()] * 2,
        out_specs=vmem_spec(),
        cost_estimate=cost(rows, width),
        compiler_params=pltpu.CompilerParams(vmem_limit_bytes=4 * 1024 * 1024),
    )(values, pltpu.with_memory_space_constraint(merge_op, pltpu.VMEM))


CHUNK = 256


def fetched_dot_kernel(values_in_hbm, sign_ref, values_ref, partner_ref, op_hbm_ref, out_ref, op_ref, own_ref, sems):
    width = op_ref.shape[0]
    blocks = width // CHUNK
    if values_in_hbm:
        own_copy = pltpu.make_async_copy(values_ref, own_ref, sems.at[blocks])
        own_copy.start()
    copies = []
    for index in range(blocks):
        rows = pl.ds(index * CHUNK, CHUNK)
        copy = pltpu.make_async_copy(op_hbm_ref.at[rows, :], op_ref.at[rows, :], sems.at[index])
        copy.start()
        copies.append(copy)
    if values_in_hbm:
        own_copy.wait()
        first = own_ref[...].astype(jnp.float32)
    else:
        first = values_ref[...].astype(jnp.float32)
    second = partner_ref[...].astype(jnp.float32)
    mixed = ((second + sign_ref[...] * first) * half_root).astype(jnp.bfloat16)
    total = jnp.zeros(out_ref.shape, jnp.float32)
    for index, copy in enumerate(copies):
        copy.wait()
        rows = slice(index * CHUNK, (index + 1) * CHUNK)
        total = total + jnp.dot(mixed[:, rows], op_ref[rows, :], preferred_element_type=jnp.float32)
    out_ref[...] = total.astype(out_ref.dtype)


def fetched_dot(sign, values, partner, merge_op, values_in_hbm):
    rows, width = values.shape
    if values_in_hbm:
        values_spec = pl.BlockSpec(memory_space=pl.ANY)
        values = pltpu.with_memory_space_constraint(values, pltpu.HBM)
    else:
        values_spec = vmem_spec()
    return pl.pallas_call(
        functools.partial(fetched_dot_kernel, values_in_hbm),
        out_shape=jax.ShapeDtypeStruct(values.shape, jnp.bfloat16),
        in_specs=[vmem_spec(), values_spec, vmem_spec(), pl.BlockSpec(memory_space=pl.ANY)],
        out_specs=vmem_spec(),
        scratch_shapes=[
            pltpu.VMEM(merge_op.shape, merge_op.dtype),
            pltpu.VMEM(values.shape, values.dtype),
            pltpu.SemaphoreType.DMA((width // CHUNK + 1,)),
        ],
        cost_estimate=cost(rows, width),
        compiler_params=pltpu.CompilerParams(vmem_limit_bytes=16 * 1024 * 1024),
    )(sign, values, partner, pltpu.with_memory_space_constraint(merge_op, pltpu.HBM))


def warm_kernel(values_ref, op_ref, out_ref):
    out_ref[...] = values_ref[0:8, 0:128].astype(jnp.float32) * 0.0


def warmed(values, merge_op):
    return pl.pallas_call(
        warm_kernel,
        out_shape=jax.ShapeDtypeStruct((8, 128), jnp.float32),
        in_specs=[vmem_spec()] * 2,
        out_specs=vmem_spec(),
        compiler_params=pltpu.CompilerParams(vmem_limit_bytes=4 * 1024 * 1024, has_side_effects=True),
    )(values, pltpu.with_memory_space_constraint(merge_op, pltpu.VMEM))


def haar_pair(values, partner, lat_index, bit_level):
    is_lower = lat_index // 2**bit_level % 2 == 0
    first = values.astype(jnp.float32)
    second = partner.astype(jnp.float32)
    return jnp.where(is_lower, (first + second) * half_root, (second - first) * half_root).astype(
        jnp.bfloat16
    )


def level_sign(lat_index, bit_level, width):
    is_lower = lat_index // 2**bit_level % 2 == 0
    return jnp.full((1, width), jnp.where(is_lower, 1.0, -1.0), jnp.float32)


def sweep_layer(leaf_data, merge_op, fetch):
    lat_count = lax.axis_size("lat")
    lat_index = lax.axis_index("lat")
    levels = lat_count.bit_length() - 1
    width = leaf_data.shape[1]
    values = leaf_data
    for bit_level in range(levels):
        if fetch and bit_level > 0:
            partner = partner_2(values, "lat", bit_level)
            warmed(values, merge_op)
        else:
            partner = partner_2(values, "lat", bit_level)
        sign = level_sign(lat_index, bit_level, width)
        if fetch and bit_level == 0:
            values = fetched_dot(sign, values, partner, merge_op, bit_level == 0)
        else:
            values = mixed_dot(sign, values, partner, merge_op)
    values = transposed_dot(values, merge_op)
    for bit_level in range(levels - 1, -1, -1):
        partner = partner_2(values, "lat", bit_level)
        values = haar_pair(values, partner, lat_index, bit_level)
    return values


def on_device(sources, coupling, merge_ops):
    merge_op = merge_ops[0, 0]
    coupling_row = coupling[0, 0]
    depth_index = lax.axis_index("depth")
    depth_count = lax.axis_size("depth")
    shot_rows = sources[0, 0]
    result = jnp.zeros_like(shot_rows)
    for sweep_step in range(depth_count):
        if sweep_step == 0:
            leaf_data = shot_rows
        else:
            leaf_data = (
                shot_rows.astype(jnp.float32) + coupling_row * incoming.astype(jnp.float32)
            ).astype(jnp.bfloat16)
        if sweep_step == 0:
            solved = sweep_layer(leaf_data, merge_op, True)
        else:
            solved = sweep_layer(leaf_data, merge_op, False)
        result = jnp.where(depth_index == sweep_step, solved, result)
        if sweep_step + 1 < depth_count:
            incoming = handed_down(solved, "depth", sweep_step)
    return result[None, None]


def solution(mesh):
    return jax.shard_map(
        on_device,
        mesh=mesh,
        in_specs=(
            P("depth", "lat", None, None),
            P("depth", "lat", None),
            P("depth", "lat", None, None),
        ),
        out_specs=P("depth", "lat", None, None),
        check_vma=False,
    )
```

profile of v0, /device:TPU:7, one launch (start us, length us, event | category | flops | bytes accessed | tf_op | source)
XLA Modules:
  0.0 183.8 jit_solution(10996211450166882737)
XLA Ops:
  0.0 0.7 collective-permute-start
  0.7 1.2 collective-permute-done.partner_ref
  1.9 3.8 %shard_map.37.values_ref = bf16[32,2048]{1,0:T(8,128)(2,1)S(1)} custom-call(f32[1,2048]{1,0:T(1,128)S(1)} %broadcast_in_dim.10.sign_ref, bf16[32,2048]{1,0:T(8,128)(2,1)} %bitcast.29, bf16[32,2048]{1,0:T(8,128)(2,1)S(1)} %collective-permute-done.partner_ref, bf16[2048,2048]{1,0:T(8,128)(2,1)} %bitcast.8), custom_call_target="tpu_custom_call" | custom-call | flops 268435456 | bytes 8781824 | tf_op jit(solution)/shard_map/pallas_call | solution.py:126
  5.7 1.4 collective-permute-start.1
  7.1 3.4 %collective-permute-done.1.partner_ref = bf16[32,2048]{1,0:T(8,128)(2,1)S(1)} collective-permute-done((bf16[32,2048]{1,0:T(8,128)(2,1)S(1)}, bf16[32,2048]{1,0:T(8,128)(2,1)S(1)}, u32[]{:S(2)}, u32[]{:S(2)}) %collective-permute-start.1) | collective-permute-done | bytes 131104 | tf_op jit(solution)/shard_map/ppermute | solution.py:22
  10.5 3.4 %copy-done = bf16[1,1,2048,2048]{3,2,1,0:T(8,128)(2,1)S(1)} copy-done((bf16[1,1,2048,2048]{3,2,1,0:T(8,128)(2,1)S(1)}, bf16[1,1,2048,2048]{3,2,1,0:T(8,128)(2,1)}, u32[]{:S(2)}) %copy-start) | copy-done | bytes 8388632
  13.9 1.5 shard_map.39.values_ref
  15.4 2.3 %collective-permute-start.2 = (bf16[32,2048]{1,0:T(8,128)(2,1)S(1)}, bf16[32,2048]{1,0:T(8,128)(2,1)S(1)}, u32[]{:S(2)}, u32[]{:S(2)}) collective-permute-start(bf16[32,2048]{1,0:T(8,128)(2,1)S(1)} %shard_map.39.values_ref), channel_id=1, source_target_pairs={{0,4},{4,0},{1,5},{5,1},{2,6},{6,2},{3,7},{7,3},{8,12},{12,8},{9,1... | collective-permute-start | bytes 393224 | tf_op jit(solution)/shard_map/ppermute | solution.py:22
  17.7 5.8 %collective-permute-done.2.partner_ref = bf16[32,2048]{1,0:T(8,128)(2,1)S(1)} collective-permute-done((bf16[32,2048]{1,0:T(8,128)(2,1)S(1)}, bf16[32,2048]{1,0:T(8,128)(2,1)S(1)}, u32[]{:S(2)}, u32[]{:S(2)}) %collective-permute-start.2) | collective-permute-done | bytes 131104 | tf_op jit(solution)/shard_map/ppermute | solution.py:22
  23.6 3.4 %copy-done.1 = bf16[1,1,2048,2048]{3,2,1,0:T(8,128)(2,1)S(1)} copy-done((bf16[1,1,2048,2048]{3,2,1,0:T(8,128)(2,1)S(1)}, bf16[1,1,2048,2048]{3,2,1,0:T(8,128)(2,1)}, u32[]{:S(2)}) %copy-start.1) | copy-done | bytes 8388632
  26.9 1.5 shard_map.41.values_ref
  28.5 2.4 %shard_map.42 = bf16[32,2048]{1,0:T(8,128)(2,1)S(1)} custom-call(bf16[32,2048]{1,0:T(8,128)(2,1)S(1)} %shard_map.41.values_ref, bf16[2048,2048]{1,0:T(8,128)(2,1)S(1)} %bitcast.11), custom_call_target="tpu_custom_call" | custom-call | flops 268435456 | bytes 8781824 | tf_op jit(solution)/shard_map/pallas_call | solution.py:79
  30.9 4.7 %collective-permute-done.3 = bf16[32,2048]{1,0:T(8,128)(2,1)S(1)} collective-permute-done((bf16[32,2048]{1,0:T(8,128)(2,1)S(1)}, bf16[32,2048]{1,0:T(8,128)(2,1)S(1)}, u32[]{:S(2)}, u32[]{:S(2)}) %collective-permute-start.3) | collective-permute-done | bytes 131104 | tf_op jit(solution)/shard_map/ppermute | solution.py:22
  35.7 2.9 %collective-permute-start.4 = (bf16[32,2048]{1,0:T(8,128)(2,1)S(1)}, bf16[32,2048]{1,0:T(8,128)(2,1)S(1)}, u32[]{:S(2)}, u32[]{:S(2)}) collective-permute-start(bf16[32,2048]{1,0:T(8,128)(2,1)S(1)} %fusion.2), channel_id=1, source_target_pairs={{0,2},{2,0},{1,3},{3,1},{4,6},{6,4},{5,7},{7,5},{8,10},{10,8},{9,1... | collective-permute-start | bytes 393224 | tf_op jit(solution)/shard_map/ppermute | solution.py:22
  38.6 2.9 %collective-permute-done.4 = bf16[32,2048]{1,0:T(8,128)(2,1)S(1)} collective-permute-done((bf16[32,2048]{1,0:T(8,128)(2,1)S(1)}, bf16[32,2048]{1,0:T(8,128)(2,1)S(1)}, u32[]{:S(2)}, u32[]{:S(2)}) %collective-permute-start.4) | collective-permute-done | bytes 131104 | tf_op jit(solution)/shard_map/ppermute | solution.py:22
  41.6 4.5 %collective-permute-start.5 = (bf16[32,2048]{1,0:T(8,128)(2,1)S(1)}, bf16[32,2048]{1,0:T(8,128)(2,1)S(1)}, u32[]{:S(2)}, u32[]{:S(2)}) collective-permute-start(bf16[32,2048]{1,0:T(8,128)(2,1)S(1)} %fusion.6), channel_id=1, source_target_pairs={{0,1},{1,0},{2,3},{3,2},{4,5},{5,4},{6,7},{7,6},{8,9},{9,8},{10,11... | collective-permute-start | bytes 393224 | tf_op jit(solution)/shard_map/ppermute | solution.py:22
  46.1 1.0 collective-permute-done.5
  47.2 0.7 collective-permute-start.6
  47.9 0.4 collective-permute-start.7
  48.4 1.0 collective-permute-done.7.partner_ref
  49.3 1.5 shard_map.43.values_ref
  50.9 4.7 %collective-permute-done.8.partner_ref = bf16[32,2048]{1,0:T(8,128)(2,1)S(1)} collective-permute-done((bf16[32,2048]{1,0:T(8,128)(2,1)S(1)}, bf16[32,2048]{1,0:T(8,128)(2,1)S(1)}, u32[]{:S(2)}, u32[]{:S(2)}) %collective-permute-start.8) | collective-permute-done | bytes 131104 | tf_op jit(solution)/shard_map/ppermute | solution.py:22
  55.6 1.5 shard_map.44.values_ref
  57.1 9.1 %collective-permute-done.9.partner_ref = bf16[32,2048]{1,0:T(8,128)(2,1)S(1)} collective-permute-done((bf16[32,2048]{1,0:T(8,128)(2,1)S(1)}, bf16[32,2048]{1,0:T(8,128)(2,1)S(1)}, u32[]{:S(2)}, u32[]{:S(2)}) %collective-permute-start.9) | collective-permute-done | bytes 131104 | tf_op jit(solution)/shard_map/ppermute | solution.py:22
  66.3 1.5 shard_map.45.values_ref
  67.8 2.4 %shard_map.46 = bf16[32,2048]{1,0:T(8,128)(2,1)S(1)} custom-call(bf16[32,2048]{1,0:T(8,128)(2,1)S(1)} %shard_map.45.values_ref, bf16[2048,2048]{1,0:T(8,128)(2,1)S(1)} %bitcast.17), custom_call_target="tpu_custom_call" | custom-call | flops 268435456 | bytes 8781824 | tf_op jit(solution)/shard_map/pallas_call | solution.py:79
  70.2 7.7 %collective-permute-done.10 = bf16[32,2048]{1,0:T(8,128)(2,1)S(1)} collective-permute-done((bf16[32,2048]{1,0:T(8,128)(2,1)S(1)}, bf16[32,2048]{1,0:T(8,128)(2,1)S(1)}, u32[]{:S(2)}, u32[]{:S(2)}) %collective-permute-start.10) | collective-permute-done | bytes 131104 | tf_op jit(solution)/shard_map/ppermute | solution.py:22
  78.0 0.1 collective-permute-start.11
  78.0 4.6 %collective-permute-done.11 = bf16[32,2048]{1,0:T(8,128)(2,1)S(1)} collective-permute-done((bf16[32,2048]{1,0:T(8,128)(2,1)S(1)}, bf16[32,2048]{1,0:T(8,128)(2,1)S(1)}, u32[]{:S(2)}, u32[]{:S(2)}) %collective-permute-start.11) | collective-permute-done | bytes 131104 | tf_op jit(solution)/shard_map/ppermute | solution.py:22
  82.7 1.4 collective-permute-start.12
  84.1 1.0 collective-permute-done.12
  85.1 0.8 collective-permute-start.13
  86.1 0.4 collective-permute-start.14
  86.5 1.0 collective-permute-done.14.partner_ref
  87.5 1.5 shard_map.47.values_ref
  89.0 4.7 %collective-permute-done.15.partner_ref = bf16[32,2048]{1,0:T(8,128)(2,1)S(1)} collective-permute-done((bf16[32,2048]{1,0:T(8,128)(2,1)S(1)}, bf16[32,2048]{1,0:T(8,128)(2,1)S(1)}, u32[]{:S(2)}, u32[]{:S(2)}) %collective-permute-start.15) | collective-permute-done | bytes 131104 | tf_op jit(solution)/shard_map/ppermute | solution.py:22
  93.7 1.5 shard_map.48.values_ref
  95.3 1.2 collective-permute-start.16
  96.4 7.9 %collective-permute-done.16.partner_ref = bf16[32,2048]{1,0:T(8,128)(2,1)S(1)} collective-permute-done((bf16[32,2048]{1,0:T(8,128)(2,1)S(1)}, bf16[32,2048]{1,0:T(8,128)(2,1)S(1)}, u32[]{:S(2)}, u32[]{:S(2)}) %collective-permute-start.16) | collective-permute-done | bytes 131104 | tf_op jit(solution)/shard_map/ppermute | solution.py:22
  104.4 1.5 shard_map.49.values_ref
  105.9 2.4 %shard_map.50 = bf16[32,2048]{1,0:T(8,128)(2,1)S(1)} custom-call(bf16[32,2048]{1,0:T(8,128)(2,1)S(1)} %shard_map.49.values_ref, bf16[2048,2048]{1,0:T(8,128)(2,1)S(1)} %bitcast.21), custom_call_target="tpu_custom_call" | custom-call | flops 268435456 | bytes 8781824 | tf_op jit(solution)/shard_map/pallas_call | solution.py:79
  108.4 8.7 %collective-permute-done.17 = bf16[32,2048]{1,0:T(8,128)(2,1)S(1)} collective-permute-done((bf16[32,2048]{1,0:T(8,128)(2,1)S(1)}, bf16[32,2048]{1,0:T(8,128)(2,1)S(1)}, u32[]{:S(2)}, u32[]{:S(2)}) %collective-permute-start.17) | collective-permute-done | bytes 131104 | tf_op jit(solution)/shard_map/ppermute | solution.py:22
  117.1 0.1 collective-permute-start.18
  117.2 4.6 %collective-permute-done.18 = bf16[32,2048]{1,0:T(8,128)(2,1)S(1)} collective-permute-done((bf16[32,2048]{1,0:T(8,128)(2,1)S(1)}, bf16[32,2048]{1,0:T(8,128)(2,1)S(1)}, u32[]{:S(2)}, u32[]{:S(2)}) %collective-permute-start.18) | collective-permute-done | bytes 131104 | tf_op jit(solution)/shard_map/ppermute | solution.py:22
  121.8 1.4 collective-permute-start.19
  123.2 1.0 collective-permute-done.19
  124.3 1.3 collective-permute-start.20
  125.6 16.1 %collective-permute-done.20 = bf16[32,2048]{1,0:T(8,128)(2,1)S(1)} collective-permute-done((bf16[32,2048]{1,0:T(8,128)(2,1)S(1)}, bf16[32,2048]{1,0:T(8,128)(2,1)S(1)}, u32[]{:S(2)}, u32[]{:S(2)}) %collective-permute-start.20) | collective-permute-done | bytes 131104 | tf_op jit(solution)/shard_map/ppermute | solution.py:26
  141.7 1.0 collective-permute-start.21
  142.8 1.0 collective-permute-done.21.partner_ref
  143.7 1.5 shard_map.51.values_ref
  145.3 4.7 %collective-permute-done.22.partner_ref = bf16[32,2048]{1,0:T(8,128)(2,1)S(1)} collective-permute-done((bf16[32,2048]{1,0:T(8,128)(2,1)S(1)}, bf16[32,2048]{1,0:T(8,128)(2,1)S(1)}, u32[]{:S(2)}, u32[]{:S(2)}) %collective-permute-start.22) | collective-permute-done | bytes 131104 | tf_op jit(solution)/shard_map/ppermute | solution.py:22
  150.0 1.5 shard_map.52.values_ref
  151.5 0.2 collective-permute-start.23
  151.7 8.5 %collective-permute-done.23.partner_ref = bf16[32,2048]{1,0:T(8,128)(2,1)S(1)} collective-permute-done((bf16[32,2048]{1,0:T(8,128)(2,1)S(1)}, bf16[32,2048]{1,0:T(8,128)(2,1)S(1)}, u32[]{:S(2)}, u32[]{:S(2)}) %collective-permute-start.23) | collective-permute-done | bytes 131104 | tf_op jit(solution)/shard_map/ppermute | solution.py:22
  160.2 1.5 shard_map.53.values_ref
  161.7 2.4 %shard_map.54 = bf16[32,2048]{1,0:T(8,128)(2,1)S(1)} custom-call(bf16[32,2048]{1,0:T(8,128)(2,1)S(1)} %shard_map.53.values_ref, bf16[2048,2048]{1,0:T(8,128)(2,1)S(1)} %bitcast.25), custom_call_target="tpu_custom_call" | custom-call | flops 268435456 | bytes 8781824 | tf_op jit(solution)/shard_map/pallas_call | solution.py:79
  164.2 8.1 %collective-permute-done.24 = bf16[32,2048]{1,0:T(8,128)(2,1)S(1)} collective-permute-done((bf16[32,2048]{1,0:T(8,128)(2,1)S(1)}, bf16[32,2048]{1,0:T(8,128)(2,1)S(1)}, u32[]{:S(2)}, u32[]{:S(2)}) %collective-permute-start.24) | collective-permute-done | bytes 131104 | tf_op jit(solution)/shard_map/ppermute | solution.py:22
  172.4 4.5 %collective-permute-done.25 = bf16[32,2048]{1,0:T(8,128)(2,1)S(1)} collective-permute-done((bf16[32,2048]{1,0:T(8,128)(2,1)S(1)}, bf16[32,2048]{1,0:T(8,128)(2,1)S(1)}, u32[]{:S(2)}, u32[]{:S(2)}) %collective-permute-start.25) | collective-permute-done | bytes 131104 | tf_op jit(solution)/shard_map/ppermute | solution.py:22
  177.1 1.4 collective-permute-start.26
  178.5 3.4 %copy-done.2 = bf16[1,1,2048,2048]{3,2,1,0:T(8,128)(2,1)S(1)} copy-done((bf16[1,1,2048,2048]{3,2,1,0:T(8,128)(2,1)S(1)}, bf16[1,1,2048,2048]{3,2,1,0:T(8,128)(2,1)}, u32[]{:S(2)}) %copy-start.2) | copy-done | bytes 8388632
  181.9 0.6 shard_map.38
  182.5 0.6 shard_map.40
  183.1 0.8 fusion.52
  (41 shorter events, 1.3 us)
Async XLA Ops:
  0.0 1.9 %collective-permute-start = (bf16[32,2048]{1,0:T(8,128)(2,1)}, bf16[32,2048]{1,0:T(8,128)(2,1)S(1)}, u32[]{:S(2)}, u32[]{:S(2)}) collective-permute-start(bf16[32,2048]{1,0:T(8,128)(2,1)} %bitcast.28), channel_id=1, source_target_pairs={{0,1},{1,0},{2,3},{3,2},{4,5},{5,4},{6,7},{7,6},{8,9},{9,8},{10,11... | collective-permute-start | bytes 393224 | tf_op jit(solution)/shard_map/ppermute | solution.py:22
  5.7 4.8 %collective-permute-start.1 = (bf16[32,2048]{1,0:T(8,128)(2,1)S(1)}, bf16[32,2048]{1,0:T(8,128)(2,1)S(1)}, u32[]{:S(2)}, u32[]{:S(2)}) collective-permute-start(bf16[32,2048]{1,0:T(8,128)(2,1)S(1)} %shard_map.37.values_ref), channel_id=1, source_target_pairs={{0,2},{2,0},{1,3},{3,1},{4,6},{6,4},{5,7},{7,5},{8,10},{10,8},{9,1... | collective-permute-start | bytes 393224 | tf_op jit(solution)/shard_map/ppermute | solution.py:22
  10.5 3.4 %copy-start = (bf16[1,1,2048,2048]{3,2,1,0:T(8,128)(2,1)S(1)}, bf16[1,1,2048,2048]{3,2,1,0:T(8,128)(2,1)}, u32[]{:S(2)}) copy-start(bf16[1,1,2048,2048]{3,2,1,0:T(8,128)(2,1)} %param.5) | copy-start | bytes 25165828
  15.4 8.1 %collective-permute-start.2 = (bf16[32,2048]{1,0:T(8,128)(2,1)S(1)}, bf16[32,2048]{1,0:T(8,128)(2,1)S(1)}, u32[]{:S(2)}, u32[]{:S(2)}) collective-permute-start(bf16[32,2048]{1,0:T(8,128)(2,1)S(1)} %shard_map.39.values_ref), channel_id=1, source_target_pairs={{0,4},{4,0},{1,5},{5,1},{2,6},{6,2},{3,7},{7,3},{8,12},{12,8},{9,1... | collective-permute-start | bytes 393224 | tf_op jit(solution)/shard_map/ppermute | solution.py:22
  23.5 3.4 %copy-start.1 = (bf16[1,1,2048,2048]{3,2,1,0:T(8,128)(2,1)S(1)}, bf16[1,1,2048,2048]{3,2,1,0:T(8,128)(2,1)}, u32[]{:S(2)}) copy-start(bf16[1,1,2048,2048]{3,2,1,0:T(8,128)(2,1)} %param.5) | copy-start | bytes 25165828
  26.9 20.9 %copy-start.3 = (bf16[1,1,32,2048]{3,2,1,0:T(8,128)(2,1)S(1)}, bf16[1,1,32,2048]{3,2,1,0:T(8,128)(2,1)}, u32[]{:S(2)}) copy-start(bf16[1,1,32,2048]{3,2,1,0:T(8,128)(2,1)} %param.3) | copy-start | bytes 393220
  26.9 20.9 %copy-start.4 = (f32[1,1,2048]{2,1,0:T(1,128)S(1)}, f32[1,1,2048]{2,1,0:T(1,128)}, u32[]{:S(2)}) copy-start(f32[1,1,2048]{2,1,0:T(1,128)} %param.4) | copy-start | bytes 24580
  26.9 22.4 %slice-start = ((s8[8388608]{0:T(1024)(128)(4,1)}), s8[4194304]{0:T(1024)(128)(4,1)S(1)}, s32[]{:S(2)}) async-start(s8[8388608]{0:T(1024)(128)(4,1)} %bitcast.12), calls=%async_computation | async-start | bytes 8388608
  28.5 20.9 %slice-start.1 = ((s8[8388608]{0:T(1024)(128)(4,1)}), s8[4194304]{0:T(1024)(128)(4,1)S(1)}, s32[]{:S(2)}) async-start(s8[8388608]{0:T(1024)(128)(4,1)} %bitcast.12), calls=%async_computation.1 | async-start | bytes 8388608
  30.8 4.8 %collective-permute-start.3 = (bf16[32,2048]{1,0:T(8,128)(2,1)S(1)}, bf16[32,2048]{1,0:T(8,128)(2,1)S(1)}, u32[]{:S(2)}, u32[]{:S(2)}) collective-permute-start(bf16[32,2048]{1,0:T(8,128)(2,1)S(1)} %shard_map.42), channel_id=1, source_target_pairs={{0,4},{4,0},{1,5},{5,1},{2,6},{6,2},{3,7},{7,3},{8,12},{12,8},{9,1... | collective-permute-start | bytes 393224 | tf_op jit(solution)/shard_map/ppermute | solution.py:22
  35.7 5.8 %collective-permute-start.4 = (bf16[32,2048]{1,0:T(8,128)(2,1)S(1)}, bf16[32,2048]{1,0:T(8,128)(2,1)S(1)}, u32[]{:S(2)}, u32[]{:S(2)}) collective-permute-start(bf16[32,2048]{1,0:T(8,128)(2,1)S(1)} %fusion.2), channel_id=1, source_target_pairs={{0,2},{2,0},{1,3},{3,1},{4,6},{6,4},{5,7},{7,5},{8,10},{10,8},{9,1... | collective-permute-start | bytes 393224 | tf_op jit(solution)/shard_map/ppermute | solution.py:22
  41.6 5.5 %collective-permute-start.5 = (bf16[32,2048]{1,0:T(8,128)(2,1)S(1)}, bf16[32,2048]{1,0:T(8,128)(2,1)S(1)}, u32[]{:S(2)}, u32[]{:S(2)}) collective-permute-start(bf16[32,2048]{1,0:T(8,128)(2,1)S(1)} %fusion.6), channel_id=1, source_target_pairs={{0,1},{1,0},{2,3},{3,2},{4,5},{5,4},{6,7},{7,6},{8,9},{9,8},{10,11... | collective-permute-start | bytes 393224 | tf_op jit(solution)/shard_map/ppermute | solution.py:22
  47.2 0.7 collective-permute-start.6
  47.9 1.4 collective-permute-start.7
  50.9 4.7 %collective-permute-start.8 = (bf16[32,2048]{1,0:T(8,128)(2,1)S(1)}, bf16[32,2048]{1,0:T(8,128)(2,1)S(1)}, u32[]{:S(2)}, u32[]{:S(2)}) collective-permute-start(bf16[32,2048]{1,0:T(8,128)(2,1)S(1)} %shard_map.43.values_ref), channel_id=1, source_target_pairs={{0,2},{2,0},{1,3},{3,1},{4,6},{6,4},{5,7},{7,5},{8,10},{10,8},{9,1... | collective-permute-start | bytes 393224 | tf_op jit(solution)/shard_map/ppermute | solution.py:22
  57.1 9.1 %collective-permute-start.9 = (bf16[32,2048]{1,0:T(8,128)(2,1)S(1)}, bf16[32,2048]{1,0:T(8,128)(2,1)S(1)}, u32[]{:S(2)}, u32[]{:S(2)}) collective-permute-start(bf16[32,2048]{1,0:T(8,128)(2,1)S(1)} %shard_map.44.values_ref), channel_id=1, source_target_pairs={{0,4},{4,0},{1,5},{5,1},{2,6},{6,2},{3,7},{7,3},{8,12},{12,8},{9,1... | collective-permute-start | bytes 393224 | tf_op jit(solution)/shard_map/ppermute | solution.py:22
  70.2 7.7 %collective-permute-start.10 = (bf16[32,2048]{1,0:T(8,128)(2,1)S(1)}, bf16[32,2048]{1,0:T(8,128)(2,1)S(1)}, u32[]{:S(2)}, u32[]{:S(2)}) collective-permute-start(bf16[32,2048]{1,0:T(8,128)(2,1)S(1)} %shard_map.46), channel_id=1, source_target_pairs={{0,4},{4,0},{1,5},{5,1},{2,6},{6,2},{3,7},{7,3},{8,12},{12,8},{9,1... | collective-permute-start | bytes 393224 | tf_op jit(solution)/shard_map/ppermute | solution.py:22
  78.0 4.6 %collective-permute-start.11 = (bf16[32,2048]{1,0:T(8,128)(2,1)S(1)}, bf16[32,2048]{1,0:T(8,128)(2,1)S(1)}, u32[]{:S(2)}, u32[]{:S(2)}) collective-permute-start(bf16[32,2048]{1,0:T(8,128)(2,1)S(1)} %fusion.14), channel_id=1, source_target_pairs={{0,2},{2,0},{1,3},{3,1},{4,6},{6,4},{5,7},{7,5},{8,10},{10,8},{9,1... | collective-permute-start | bytes 393224 | tf_op jit(solution)/shard_map/ppermute | solution.py:22
  82.7 2.4 %collective-permute-start.12 = (bf16[32,2048]{1,0:T(8,128)(2,1)S(1)}, bf16[32,2048]{1,0:T(8,128)(2,1)S(1)}, u32[]{:S(2)}, u32[]{:S(2)}) collective-permute-start(bf16[32,2048]{1,0:T(8,128)(2,1)S(1)} %fusion.18), channel_id=1, source_target_pairs={{0,1},{1,0},{2,3},{3,2},{4,5},{5,4},{6,7},{7,6},{8,9},{9,8},{10,11... | collective-permute-start | bytes 393224 | tf_op jit(solution)/shard_map/ppermute | solution.py:22
  85.1 0.9 collective-permute-start.13
  86.1 1.4 collective-permute-start.14
  89.0 4.7 %collective-permute-start.15 = (bf16[32,2048]{1,0:T(8,128)(2,1)S(1)}, bf16[32,2048]{1,0:T(8,128)(2,1)S(1)}, u32[]{:S(2)}, u32[]{:S(2)}) collective-permute-start(bf16[32,2048]{1,0:T(8,128)(2,1)S(1)} %shard_map.47.values_ref), channel_id=1, source_target_pairs={{0,2},{2,0},{1,3},{3,1},{4,6},{6,4},{5,7},{7,5},{8,10},{10,8},{9,1... | collective-permute-start | bytes 393224 | tf_op jit(solution)/shard_map/ppermute | solution.py:22
  95.3 9.1 %collective-permute-start.16 = (bf16[32,2048]{1,0:T(8,128)(2,1)S(1)}, bf16[32,2048]{1,0:T(8,128)(2,1)S(1)}, u32[]{:S(2)}, u32[]{:S(2)}) collective-permute-start(bf16[32,2048]{1,0:T(8,128)(2,1)S(1)} %shard_map.48.values_ref), channel_id=1, source_target_pairs={{0,4},{4,0},{1,5},{5,1},{2,6},{6,2},{3,7},{7,3},{8,12},{12,8},{9,1... | collective-permute-start | bytes 393224 | tf_op jit(solution)/shard_map/ppermute | solution.py:22
  108.3 8.7 %collective-permute-start.17 = (bf16[32,2048]{1,0:T(8,128)(2,1)S(1)}, bf16[32,2048]{1,0:T(8,128)(2,1)S(1)}, u32[]{:S(2)}, u32[]{:S(2)}) collective-permute-start(bf16[32,2048]{1,0:T(8,128)(2,1)S(1)} %shard_map.50), channel_id=1, source_target_pairs={{0,4},{4,0},{1,5},{5,1},{2,6},{6,2},{3,7},{7,3},{8,12},{12,8},{9,1... | collective-permute-start | bytes 393224 | tf_op jit(solution)/shard_map/ppermute | solution.py:22
  117.1 4.6 %collective-permute-start.18 = (bf16[32,2048]{1,0:T(8,128)(2,1)S(1)}, bf16[32,2048]{1,0:T(8,128)(2,1)S(1)}, u32[]{:S(2)}, u32[]{:S(2)}) collective-permute-start(bf16[32,2048]{1,0:T(8,128)(2,1)S(1)} %fusion.26), channel_id=1, source_target_pairs={{0,2},{2,0},{1,3},{3,1},{4,6},{6,4},{5,7},{7,5},{8,10},{10,8},{9,1... | collective-permute-start | bytes 393224 | tf_op jit(solution)/shard_map/ppermute | solution.py:22
  121.8 2.4 %collective-permute-start.19 = (bf16[32,2048]{1,0:T(8,128)(2,1)S(1)}, bf16[32,2048]{1,0:T(8,128)(2,1)S(1)}, u32[]{:S(2)}, u32[]{:S(2)}) collective-permute-start(bf16[32,2048]{1,0:T(8,128)(2,1)S(1)} %fusion.30), channel_id=1, source_target_pairs={{0,1},{1,0},{2,3},{3,2},{4,5},{5,4},{6,7},{7,6},{8,9},{9,8},{10,11... | collective-permute-start | bytes 393224 | tf_op jit(solution)/shard_map/ppermute | solution.py:22
  124.3 17.4 %collective-permute-start.20 = (bf16[32,2048]{1,0:T(8,128)(2,1)S(1)}, bf16[32,2048]{1,0:T(8,128)(2,1)S(1)}, u32[]{:S(2)}, u32[]{:S(2)}) collective-permute-start(bf16[32,2048]{1,0:T(8,128)(2,1)S(1)} %fusion.34), channel_id=1, source_target_pairs={{16,24},{17,25},{18,26},{19,27},{20,28},{21,29},{22,30},{23,31}} | collective-permute-start | bytes 393224 | tf_op jit(solution)/shard_map/ppermute | solution.py:26
  141.7 2.0 %collective-permute-start.21 = (bf16[32,2048]{1,0:T(8,128)(2,1)S(1)}, bf16[32,2048]{1,0:T(8,128)(2,1)S(1)}, u32[]{:S(2)}, u32[]{:S(2)}) collective-permute-start(bf16[32,2048]{1,0:T(8,128)(2,1)S(1)} %fusion.50.values_ref), channel_id=1, source_target_pairs={{0,1},{1,0},{2,3},{3,2},{4,5},{5,4},{6,7},{7,6},{8,9},{9,8},{10,11... | collective-permute-start | bytes 393224 | tf_op jit(solution)/shard_map/ppermute | solution.py:22
  145.3 4.7 %collective-permute-start.22 = (bf16[32,2048]{1,0:T(8,128)(2,1)S(1)}, bf16[32,2048]{1,0:T(8,128)(2,1)S(1)}, u32[]{:S(2)}, u32[]{:S(2)}) collective-permute-start(bf16[32,2048]{1,0:T(8,128)(2,1)S(1)} %shard_map.51.values_ref), channel_id=1, source_target_pairs={{0,2},{2,0},{1,3},{3,1},{4,6},{6,4},{5,7},{7,5},{8,10},{10,8},{9,1... | collective-permute-start | bytes 393224 | tf_op jit(solution)/shard_map/ppermute | solution.py:22
  151.5 8.7 %collective-permute-start.23 = (bf16[32,2048]{1,0:T(8,128)(2,1)S(1)}, bf16[32,2048]{1,0:T(8,128)(2,1)S(1)}, u32[]{:S(2)}, u32[]{:S(2)}) collective-permute-start(bf16[32,2048]{1,0:T(8,128)(2,1)S(1)} %shard_map.52.values_ref), channel_id=1, source_target_pairs={{0,4},{4,0},{1,5},{5,1},{2,6},{6,2},{3,7},{7,3},{8,12},{12,8},{9,1... | collective-permute-start | bytes 393224 | tf_op jit(solution)/shard_map/ppermute | solution.py:22
  164.1 8.2 %collective-permute-start.24 = (bf16[32,2048]{1,0:T(8,128)(2,1)S(1)}, bf16[32,2048]{1,0:T(8,128)(2,1)S(1)}, u32[]{:S(2)}, u32[]{:S(2)}) collective-permute-start(bf16[32,2048]{1,0:T(8,128)(2,1)S(1)} %shard_map.54), channel_id=1, source_target_pairs={{0,4},{4,0},{1,5},{5,1},{2,6},{6,2},{3,7},{7,3},{8,12},{12,8},{9,1... | collective-permute-start | bytes 393224 | tf_op jit(solution)/shard_map/ppermute | solution.py:22
  172.4 4.6 %collective-permute-start.25 = (bf16[32,2048]{1,0:T(8,128)(2,1)S(1)}, bf16[32,2048]{1,0:T(8,128)(2,1)S(1)}, u32[]{:S(2)}, u32[]{:S(2)}) collective-permute-start(bf16[32,2048]{1,0:T(8,128)(2,1)S(1)} %fusion.38), channel_id=1, source_target_pairs={{0,2},{2,0},{1,3},{3,1},{4,6},{6,4},{5,7},{7,5},{8,10},{10,8},{9,1... | collective-permute-start | bytes 393224 | tf_op jit(solution)/shard_map/ppermute | solution.py:22
  177.1 6.0 %collective-permute-start.26 = (bf16[32,2048]{1,0:T(8,128)(2,1)S(1)}, bf16[32,2048]{1,0:T(8,128)(2,1)S(1)}, u32[]{:S(2)}, u32[]{:S(2)}) collective-permute-start(bf16[32,2048]{1,0:T(8,128)(2,1)S(1)} %fusion.42), channel_id=1, source_target_pairs={{0,1},{1,0},{2,3},{3,2},{4,5},{5,4},{6,7},{7,6},{8,9},{9,8},{10,11... | collective-permute-start | bytes 393224 | tf_op jit(solution)/shard_map/ppermute | solution.py:22
  178.5 3.4 %copy-start.2 = (bf16[1,1,2048,2048]{3,2,1,0:T(8,128)(2,1)S(1)}, bf16[1,1,2048,2048]{3,2,1,0:T(8,128)(2,1)}, u32[]{:S(2)}) copy-start(bf16[1,1,2048,2048]{3,2,1,0:T(8,128)(2,1)} %param.5) | copy-start | bytes 25165828
where the time goes:
time: 184 us
  waiting for transfers between devices  118 us (64%)
  Pallas kernels  31.4 us (17%)
  starting transfers between devices  22.6 us (12%)
  local copies, waits for them, and re-layouts  10.2 us (6%)
    ppermute x24, waiting for transfers between devices, partner_2(): return lax.ppermute(block, axis, route)  102 us
    ppermute x24, starting transfers between devices, partner_2(): return lax.ppermute(block, axis, route)  19.7 us
    pallas_call x11, Pallas kernels, mixed_dot(): pl.pallas_call(mixed_dot_kernel, out_shape=jax.ShapeDtypeStruct(values.sh...  16.8 us
    ppermute x3, waiting for transfers between devices, handed_down(): return lax.ppermute(array, axis, [(layer, layer + 1)])  16.1 us
    unnamed x14, local copies, waits for them, and re-layouts  10.2 us
    pallas_call x4, Pallas kernels, transposed_dot(): pl.pallas_call(transposed_dot_kernel, out_shape=jax.ShapeDtypeStruct(valu...  9.54 us
    pallas_call x1, Pallas kernels, fetched_dot(): pl.pallas_call(functools.partial(fetched_dot_kernel, values_in_hbm), out_...  3.84 us
  transfers between devices with their start and end apart: 27, of which 24 were waited for; matrix products, arithmetic and copies ran while one was open for 0% of the time, Pallas kernels for 1%

commit v1 on v0

--- a/solution.py
+++ b/solution.py
@@ -86,7 +86,7 @@
     )(values, pltpu.with_memory_space_constraint(merge_op, pltpu.VMEM))
 
 
-CHUNK = 256
+CHUNK = 128
 
 
 def fetched_dot_kernel(values_in_hbm, sign_ref, values_ref, partner_ref, op_hbm_ref, out_ref, op_ref, own_ref, sems):
@@ -173,13 +173,13 @@
     width = leaf_data.shape[1]
     values = leaf_data
     for bit_level in range(levels):
-        if fetch and bit_level > 0:
+        if fetch and bit_level == levels - 1:
             partner = partner_2(values, "lat", bit_level)
             warmed(values, merge_op)
         else:
             partner = partner_2(values, "lat", bit_level)
         sign = level_sign(lat_index, bit_level, width)
-        if fetch and bit_level == 0:
+        if fetch and bit_level < levels - 1:
             values = fetched_dot(sign, values, partner, merge_op, bit_level == 0)
         else:
             values = mixed_dot(sign, values, partner, merge_op)

time: 184 us -> 182 us (0.989)
  local copies, waits for them, and re-layouts: 10.2 us -> 6.79 us
    pallas_call x1 -> x2, Pallas kernels: 3.84 us -> 7.53 us  [fetched_dot(): pl.pallas_call(functools.partial(fetched_dot_kernel, values_in_hbm), out_...]
    unnamed x14 -> x12, local copies, waits for them, and re-layouts: 10.2 us -> 6.77 us
    pallas_call x11 -> x10, Pallas kernels: 16.8 us -> 15.3 us  [mixed_dot(): pl.pallas_call(mixed_dot_kernel, out_shape=jax.ShapeDtypeStruct(values.sh...]
  transfers between devices with their start and end apart: 27 -> 27, of which waited for: 24 -> 24; matrix products, arithmetic and copies ran while one was open for 0% -> 0% of each run, Pallas kernels for 1% -> 0%
where the time goes in v1:
time: 182 us
  waiting for transfers between devices  118 us (65%)
  Pallas kernels  33 us (18%)
  starting transfers between devices  22.6 us (12%)
  local copies, waits for them, and re-layouts  6.79 us (4%)
    ppermute x24, waiting for transfers between devices, partner_2(): return lax.ppermute(block, axis, route)  102 us
    ppermute x24, starting transfers between devices, partner_2(): return lax.ppermute(block, axis, route)  19.8 us
    ppermute x3, waiting for transfers between devices, handed_down(): return lax.ppermute(array, axis, [(layer, layer + 1)])  16.1 us
    pallas_call x10, Pallas kernels, mixed_dot(): pl.pallas_call(mixed_dot_kernel, out_shape=jax.ShapeDtypeStruct(values.sh...  15.3 us
    pallas_call x4, Pallas kernels, transposed_dot(): pl.pallas_call(transposed_dot_kernel, out_shape=jax.ShapeDtypeStruct(valu...  9.54 us
    pallas_call x2, Pallas kernels, fetched_dot(): pl.pallas_call(functools.partial(fetched_dot_kernel, values_in_hbm), out_...  7.53 us
    unnamed x12, local copies, waits for them, and re-layouts  6.77 us
  transfers between devices with their start and end apart: 27, of which 24 were waited for; matrix products, arithmetic and copies ran while one was open for 0% of the time, Pallas kernels for 0%

profile of v1, /device:TPU:7, one launch (start us, length us, event | category | flops | bytes accessed | tf_op | source)
XLA Modules:
  0.0 182.1 jit_solution(17500997131384179705)
XLA Ops:
  0.0 0.7 collective-permute-start
  0.7 1.2 collective-permute-done.partner_ref
  1.9 3.8 %shard_map.37.values_ref = bf16[32,2048]{1,0:T(8,128)(2,1)S(1)} custom-call(f32[1,2048]{1,0:T(1,128)S(1)} %broadcast_in_dim.11.sign_ref, bf16[32,2048]{1,0:T(8,128)(2,1)} %bitcast.28, bf16[32,2048]{1,0:T(8,128)(2,1)S(1)} %collective-permute-done.partner_ref, bf16[2048,2048]{1,0:T(8,128)(2,1)} %bitcast.8), custom_call_target="tpu_custom_call" | custom-call | flops 268435456 | bytes 8781824 | tf_op jit(solution)/shard_map/pallas_call | solution.py:126
  5.7 1.4 collective-permute-start.1
  7.0 3.4 %collective-permute-done.1.partner_ref = bf16[32,2048]{1,0:T(8,128)(2,1)S(1)} collective-permute-done((bf16[32,2048]{1,0:T(8,128)(2,1)S(1)}, bf16[32,2048]{1,0:T(8,128)(2,1)S(1)}, u32[]{:S(2)}, u32[]{:S(2)}) %collective-permute-start.1) | collective-permute-done | bytes 131104 | tf_op jit(solution)/shard_map/ppermute | solution.py:22
  10.5 3.7 %shard_map.38.values_ref = bf16[32,2048]{1,0:T(8,128)(2,1)S(1)} custom-call(f32[1,2048]{1,0:T(1,128)S(1)} %broadcast_in_dim.10.sign_ref, bf16[32,2048]{1,0:T(8,128)(2,1)S(1)} %shard_map.37.values_ref, bf16[32,2048]{1,0:T(8,128)(2,1)S(1)} %collective-permute-done.1.partner_ref, bf16[2048,2048]{1,0:T(8,128)(2,1)} %bitcast.9), custom_call_target="tpu_custom_call" | custom-call | flops 268435456 | bytes 8781824 | tf_op jit(solution)/shard_map/pallas_call | solution.py:126
  14.2 2.4 %collective-permute-start.2 = (bf16[32,2048]{1,0:T(8,128)(2,1)S(1)}, bf16[32,2048]{1,0:T(8,128)(2,1)S(1)}, u32[]{:S(2)}, u32[]{:S(2)}) collective-permute-start(bf16[32,2048]{1,0:T(8,128)(2,1)S(1)} %shard_map.38.values_ref), channel_id=1, source_target_pairs={{0,4},{4,0},{1,5},{5,1},{2,6},{6,2},{3,7},{7,3},{8,12},{12,8},{9,1... | collective-permute-start | bytes 393224 | tf_op jit(solution)/shard_map/ppermute | solution.py:22
  16.6 5.8 %collective-permute-done.2.partner_ref = bf16[32,2048]{1,0:T(8,128)(2,1)S(1)} collective-permute-done((bf16[32,2048]{1,0:T(8,128)(2,1)S(1)}, bf16[32,2048]{1,0:T(8,128)(2,1)S(1)}, u32[]{:S(2)}, u32[]{:S(2)}) %collective-permute-start.2) | collective-permute-done | bytes 131104 | tf_op jit(solution)/shard_map/ppermute | solution.py:22
  22.4 3.4 %copy-done = bf16[1,1,2048,2048]{3,2,1,0:T(8,128)(2,1)S(1)} copy-done((bf16[1,1,2048,2048]{3,2,1,0:T(8,128)(2,1)S(1)}, bf16[1,1,2048,2048]{3,2,1,0:T(8,128)(2,1)}, u32[]{:S(2)}) %copy-start) | copy-done | bytes 8388632
  25.8 1.5 shard_map.40.values_ref
  27.3 2.4 %shard_map.41 = bf16[32,2048]{1,0:T(8,128)(2,1)S(1)} custom-call(bf16[32,2048]{1,0:T(8,128)(2,1)S(1)} %shard_map.40.values_ref, bf16[2048,2048]{1,0:T(8,128)(2,1)S(1)} %bitcast.11), custom_call_target="tpu_custom_call" | custom-call | flops 268435456 | bytes 8781824 | tf_op jit(solution)/shard_map/pallas_call | solution.py:79
  29.7 4.7 %collective-permute-done.3 = bf16[32,2048]{1,0:T(8,128)(2,1)S(1)} collective-permute-done((bf16[32,2048]{1,0:T(8,128)(2,1)S(1)}, bf16[32,2048]{1,0:T(8,128)(2,1)S(1)}, u32[]{:S(2)}, u32[]{:S(2)}) %collective-permute-start.3) | collective-permute-done | bytes 131104 | tf_op jit(solution)/shard_map/ppermute | solution.py:22
  34.4 0.1 fusion.2
  34.5 2.9 %collective-permute-start.4 = (bf16[32,2048]{1,0:T(8,128)(2,1)S(1)}, bf16[32,2048]{1,0:T(8,128)(2,1)S(1)}, u32[]{:S(2)}, u32[]{:S(2)}) collective-permute-start(bf16[32,2048]{1,0:T(8,128)(2,1)S(1)} %fusion.2), channel_id=1, source_target_pairs={{0,2},{2,0},{1,3},{3,1},{4,6},{6,4},{5,7},{7,5},{8,10},{10,8},{9,1... | collective-permute-start | bytes 393224 | tf_op jit(solution)/shard_map/ppermute | solution.py:22
  37.4 2.9 %collective-permute-done.4 = bf16[32,2048]{1,0:T(8,128)(2,1)S(1)} collective-permute-done((bf16[32,2048]{1,0:T(8,128)(2,1)S(1)}, bf16[32,2048]{1,0:T(8,128)(2,1)S(1)}, u32[]{:S(2)}, u32[]{:S(2)}) %collective-permute-start.4) | collective-permute-done | bytes 131104 | tf_op jit(solution)/shard_map/ppermute | solution.py:22
  40.4 4.5 %collective-permute-start.5 = (bf16[32,2048]{1,0:T(8,128)(2,1)S(1)}, bf16[32,2048]{1,0:T(8,128)(2,1)S(1)}, u32[]{:S(2)}, u32[]{:S(2)}) collective-permute-start(bf16[32,2048]{1,0:T(8,128)(2,1)S(1)} %fusion.6), channel_id=1, source_target_pairs={{0,1},{1,0},{2,3},{3,2},{4,5},{5,4},{6,7},{7,6},{8,9},{9,8},{10,11... | collective-permute-start | bytes 393224 | tf_op jit(solution)/shard_map/ppermute | solution.py:22
  44.9 1.0 collective-permute-done.5
  46.0 0.7 collective-permute-start.6
  46.7 0.4 collective-permute-start.7
  47.2 1.0 collective-permute-done.7.partner_ref
  48.2 1.5 shard_map.42.values_ref
  49.7 4.7 %collective-permute-done.8.partner_ref = bf16[32,2048]{1,0:T(8,128)(2,1)S(1)} collective-permute-done((bf16[32,2048]{1,0:T(8,128)(2,1)S(1)}, bf16[32,2048]{1,0:T(8,128)(2,1)S(1)}, u32[]{:S(2)}, u32[]{:S(2)}) %collective-permute-start.8) | collective-permute-done | bytes 131104 | tf_op jit(solution)/shard_map/ppermute | solution.py:22
  54.4 1.5 shard_map.43.values_ref
  56.0 9.1 %collective-permute-done.9.partner_ref = bf16[32,2048]{1,0:T(8,128)(2,1)S(1)} collective-permute-done((bf16[32,2048]{1,0:T(8,128)(2,1)S(1)}, bf16[32,2048]{1,0:T(8,128)(2,1)S(1)}, u32[]{:S(2)}, u32[]{:S(2)}) %collective-permute-start.9) | collective-permute-done | bytes 131104 | tf_op jit(solution)/shard_map/ppermute | solution.py:22
  65.1 1.5 shard_map.44.values_ref
  66.6 2.4 %shard_map.45 = bf16[32,2048]{1,0:T(8,128)(2,1)S(1)} custom-call(bf16[32,2048]{1,0:T(8,128)(2,1)S(1)} %shard_map.44.values_ref, bf16[2048,2048]{1,0:T(8,128)(2,1)S(1)} %bitcast.17), custom_call_target="tpu_custom_call" | custom-call | flops 268435456 | bytes 8781824 | tf_op jit(solution)/shard_map/pallas_call | solution.py:79
  69.1 7.7 %collective-permute-done.10 = bf16[32,2048]{1,0:T(8,128)(2,1)S(1)} collective-permute-done((bf16[32,2048]{1,0:T(8,128)(2,1)S(1)}, bf16[32,2048]{1,0:T(8,128)(2,1)S(1)}, u32[]{:S(2)}, u32[]{:S(2)}) %collective-permute-start.10) | collective-permute-done | bytes 131104 | tf_op jit(solution)/shard_map/ppermute | solution.py:22
  76.8 0.1 collective-permute-start.11
  76.9 4.6 %collective-permute-done.11 = bf16[32,2048]{1,0:T(8,128)(2,1)S(1)} collective-permute-done((bf16[32,2048]{1,0:T(8,128)(2,1)S(1)}, bf16[32,2048]{1,0:T(8,128)(2,1)S(1)}, u32[]{:S(2)}, u32[]{:S(2)}) %collective-permute-start.11) | collective-permute-done | bytes 131104 | tf_op jit(solution)/shard_map/ppermute | solution.py:22
  81.5 1.4 collective-permute-start.12
  82.9 1.0 collective-permute-done.12
  84.0 0.8 collective-permute-start.13
  84.9 0.4 collective-permute-start.14
  85.3 1.0 collective-permute-done.14.partner_ref
  86.3 1.5 shard_map.46.values_ref
  87.9 4.7 %collective-permute-done.15.partner_ref = bf16[32,2048]{1,0:T(8,128)(2,1)S(1)} collective-permute-done((bf16[32,2048]{1,0:T(8,128)(2,1)S(1)}, bf16[32,2048]{1,0:T(8,128)(2,1)S(1)}, u32[]{:S(2)}, u32[]{:S(2)}) %collective-permute-start.15) | collective-permute-done | bytes 131104 | tf_op jit(solution)/shard_map/ppermute | solution.py:22
  92.6 1.5 shard_map.47.values_ref
  94.1 1.2 collective-permute-start.16
  95.3 7.9 %collective-permute-done.16.partner_ref = bf16[32,2048]{1,0:T(8,128)(2,1)S(1)} collective-permute-done((bf16[32,2048]{1,0:T(8,128)(2,1)S(1)}, bf16[32,2048]{1,0:T(8,128)(2,1)S(1)}, u32[]{:S(2)}, u32[]{:S(2)}) %collective-permute-start.16) | collective-permute-done | bytes 131104 | tf_op jit(solution)/shard_map/ppermute | solution.py:22
  103.2 1.5 shard_map.48.values_ref
  104.8 2.4 %shard_map.49 = bf16[32,2048]{1,0:T(8,128)(2,1)S(1)} custom-call(bf16[32,2048]{1,0:T(8,128)(2,1)S(1)} %shard_map.48.values_ref, bf16[2048,2048]{1,0:T(8,128)(2,1)S(1)} %bitcast.21), custom_call_target="tpu_custom_call" | custom-call | flops 268435456 | bytes 8781824 | tf_op jit(solution)/shard_map/pallas_call | solution.py:79
  107.2 8.7 %collective-permute-done.17 = bf16[32,2048]{1,0:T(8,128)(2,1)S(1)} collective-permute-done((bf16[32,2048]{1,0:T(8,128)(2,1)S(1)}, bf16[32,2048]{1,0:T(8,128)(2,1)S(1)}, u32[]{:S(2)}, u32[]{:S(2)}) %collective-permute-start.17) | collective-permute-done | bytes 131104 | tf_op jit(solution)/shard_map/ppermute | solution.py:22
  116.0 0.1 collective-permute-start.18
  116.0 4.6 %collective-permute-done.18 = bf16[32,2048]{1,0:T(8,128)(2,1)S(1)} collective-permute-done((bf16[32,2048]{1,0:T(8,128)(2,1)S(1)}, bf16[32,2048]{1,0:T(8,128)(2,1)S(1)}, u32[]{:S(2)}, u32[]{:S(2)}) %collective-permute-start.18) | collective-permute-done | bytes 131104 | tf_op jit(solution)/shard_map/ppermute | solution.py:22
  120.7 1.4 collective-permute-start.19
  122.1 1.0 collective-permute-done.19
  123.1 1.3 collective-permute-start.20
  124.4 16.1 %collective-permute-done.20 = bf16[32,2048]{1,0:T(8,128)(2,1)S(1)} collective-permute-done((bf16[32,2048]{1,0:T(8,128)(2,1)S(1)}, bf16[32,2048]{1,0:T(8,128)(2,1)S(1)}, u32[]{:S(2)}, u32[]{:S(2)}) %collective-permute-start.20) | collective-permute-done | bytes 131104 | tf_op jit(solution)/shard_map/ppermute | solution.py:26
  140.6 1.0 collective-permute-start.21
  141.6 1.0 collective-permute-done.21.partner_ref
  142.6 1.5 shard_map.50.values_ref
  144.1 4.7 %collective-permute-done.22.partner_ref = bf16[32,2048]{1,0:T(8,128)(2,1)S(1)} collective-permute-done((bf16[32,2048]{1,0:T(8,128)(2,1)S(1)}, bf16[32,2048]{1,0:T(8,128)(2,1)S(1)}, u32[]{:S(2)}, u32[]{:S(2)}) %collective-permute-start.22) | collective-permute-done | bytes 131104 | tf_op jit(solution)/shard_map/ppermute | solution.py:22
  148.8 1.5 shard_map.51.values_ref
  150.3 0.2 collective-permute-start.23
  150.5 8.5 %collective-permute-done.23.partner_ref = bf16[32,2048]{1,0:T(8,128)(2,1)S(1)} collective-permute-done((bf16[32,2048]{1,0:T(8,128)(2,1)S(1)}, bf16[32,2048]{1,0:T(8,128)(2,1)S(1)}, u32[]{:S(2)}, u32[]{:S(2)}) %collective-permute-start.23) | collective-permute-done | bytes 131104 | tf_op jit(solution)/shard_map/ppermute | solution.py:22
  159.0 1.5 shard_map.52.values_ref
  160.6 2.4 %shard_map.53 = bf16[32,2048]{1,0:T(8,128)(2,1)S(1)} custom-call(bf16[32,2048]{1,0:T(8,128)(2,1)S(1)} %shard_map.52.values_ref, bf16[2048,2048]{1,0:T(8,128)(2,1)S(1)} %bitcast.25), custom_call_target="tpu_custom_call" | custom-call | flops 268435456 | bytes 8781824 | tf_op jit(solution)/shard_map/pallas_call | solution.py:79
  163.0 8.1 %collective-permute-done.24 = bf16[32,2048]{1,0:T(8,128)(2,1)S(1)} collective-permute-done((bf16[32,2048]{1,0:T(8,128)(2,1)S(1)}, bf16[32,2048]{1,0:T(8,128)(2,1)S(1)}, u32[]{:S(2)}, u32[]{:S(2)}) %collective-permute-start.24) | collective-permute-done | bytes 131104 | tf_op jit(solution)/shard_map/ppermute | solution.py:22
  171.2 0.1 collective-permute-start.25
  171.3 4.5 %collective-permute-done.25 = bf16[32,2048]{1,0:T(8,128)(2,1)S(1)} collective-permute-done((bf16[32,2048]{1,0:T(8,128)(2,1)S(1)}, bf16[32,2048]{1,0:T(8,128)(2,1)S(1)}, u32[]{:S(2)}, u32[]{:S(2)}) %collective-permute-start.25) | collective-permute-done | bytes 131104 | tf_op jit(solution)/shard_map/ppermute | solution.py:22
  175.9 1.4 collective-permute-start.26
  177.3 3.4 %copy-done.1 = bf16[1,1,2048,2048]{3,2,1,0:T(8,128)(2,1)S(1)} copy-done((bf16[1,1,2048,2048]{3,2,1,0:T(8,128)(2,1)S(1)}, bf16[1,1,2048,2048]{3,2,1,0:T(8,128)(2,1)}, u32[]{:S(2)}) %copy-start.1) | copy-done | bytes 8388632
  180.7 0.6 shard_map.39
  181.3 0.8 fusion.52
  (38 shorter events, 1.2 us)
Async XLA Ops:
  0.0 1.9 %collective-permute-start = (bf16[32,2048]{1,0:T(8,128)(2,1)}, bf16[32,2048]{1,0:T(8,128)(2,1)S(1)}, u32[]{:S(2)}, u32[]{:S(2)}) collective-permute-start(bf16[32,2048]{1,0:T(8,128)(2,1)} %bitcast.27), channel_id=1, source_target_pairs={{0,1},{1,0},{2,3},{3,2},{4,5},{5,4},{6,7},{7,6},{8,9},{9,8},{10,11... | collective-permute-start | bytes 393224 | tf_op jit(solution)/shard_map/ppermute | solution.py:22
  5.7 4.8 %collective-permute-start.1 = (bf16[32,2048]{1,0:T(8,128)(2,1)S(1)}, bf16[32,2048]{1,0:T(8,128)(2,1)S(1)}, u32[]{:S(2)}, u32[]{:S(2)}) collective-permute-start(bf16[32,2048]{1,0:T(8,128)(2,1)S(1)} %shard_map.37.values_ref), channel_id=1, source_target_pairs={{0,2},{2,0},{1,3},{3,1},{4,6},{6,4},{5,7},{7,5},{8,10},{10,8},{9,1... | collective-permute-start | bytes 393224 | tf_op jit(solution)/shard_map/ppermute | solution.py:22
  14.2 8.2 %collective-permute-start.2 = (bf16[32,2048]{1,0:T(8,128)(2,1)S(1)}, bf16[32,2048]{1,0:T(8,128)(2,1)S(1)}, u32[]{:S(2)}, u32[]{:S(2)}) collective-permute-start(bf16[32,2048]{1,0:T(8,128)(2,1)S(1)} %shard_map.38.values_ref), channel_id=1, source_target_pairs={{0,4},{4,0},{1,5},{5,1},{2,6},{6,2},{3,7},{7,3},{8,12},{12,8},{9,1... | collective-permute-start | bytes 393224 | tf_op jit(solution)/shard_map/ppermute | solution.py:22
  22.4 3.4 %copy-start = (bf16[1,1,2048,2048]{3,2,1,0:T(8,128)(2,1)S(1)}, bf16[1,1,2048,2048]{3,2,1,0:T(8,128)(2,1)}, u32[]{:S(2)}) copy-start(bf16[1,1,2048,2048]{3,2,1,0:T(8,128)(2,1)} %param.5) | copy-start | bytes 25165828
  25.8 20.9 %copy-start.2 = (bf16[1,1,32,2048]{3,2,1,0:T(8,128)(2,1)S(1)}, bf16[1,1,32,2048]{3,2,1,0:T(8,128)(2,1)}, u32[]{:S(2)}) copy-start(bf16[1,1,32,2048]{3,2,1,0:T(8,128)(2,1)} %param.3) | copy-start | bytes 393220
  25.8 20.9 %copy-start.3 = (f32[1,1,2048]{2,1,0:T(1,128)S(1)}, f32[1,1,2048]{2,1,0:T(1,128)}, u32[]{:S(2)}) copy-start(f32[1,1,2048]{2,1,0:T(1,128)} %param.4) | copy-start | bytes 24580
  25.8 22.4 %slice-start = ((s8[8388608]{0:T(1024)(128)(4,1)}), s8[4194304]{0:T(1024)(128)(4,1)S(1)}, s32[]{:S(2)}) async-start(s8[8388608]{0:T(1024)(128)(4,1)} %bitcast.12), calls=%async_computation | async-start | bytes 8388608
  27.3 20.9 %slice-start.1 = ((s8[8388608]{0:T(1024)(128)(4,1)}), s8[4194304]{0:T(1024)(128)(4,1)S(1)}, s32[]{:S(2)}) async-start(s8[8388608]{0:T(1024)(128)(4,1)} %bitcast.12), calls=%async_computation.1 | async-start | bytes 8388608
  29.7 4.8 %collective-permute-start.3 = (bf16[32,2048]{1,0:T(8,128)(2,1)S(1)}, bf16[32,2048]{1,0:T(8,128)(2,1)S(1)}, u32[]{:S(2)}, u32[]{:S(2)}) collective-permute-start(bf16[32,2048]{1,0:T(8,128)(2,1)S(1)} %shard_map.41), channel_id=1, source_target_pairs={{0,4},{4,0},{1,5},{5,1},{2,6},{6,2},{3,7},{7,3},{8,12},{12,8},{9,1... | collective-permute-start | bytes 393224 | tf_op jit(solution)/shard_map/ppermute | solution.py:22
  34.5 5.8 %collective-permute-start.4 = (bf16[32,2048]{1,0:T(8,128)(2,1)S(1)}, bf16[32,2048]{1,0:T(8,128)(2,1)S(1)}, u32[]{:S(2)}, u32[]{:S(2)}) collective-permute-start(bf16[32,2048]{1,0:T(8,128)(2,1)S(1)} %fusion.2), channel_id=1, source_target_pairs={{0,2},{2,0},{1,3},{3,1},{4,6},{6,4},{5,7},{7,5},{8,10},{10,8},{9,1... | collective-permute-start | bytes 393224 | tf_op jit(solution)/shard_map/ppermute | solution.py:22
  40.4 5.5 %collective-permute-start.5 = (bf16[32,2048]{1,0:T(8,128)(2,1)S(1)}, bf16[32,2048]{1,0:T(8,128)(2,1)S(1)}, u32[]{:S(2)}, u32[]{:S(2)}) collective-permute-start(bf16[32,2048]{1,0:T(8,128)(2,1)S(1)} %fusion.6), channel_id=1, source_target_pairs={{0,1},{1,0},{2,3},{3,2},{4,5},{5,4},{6,7},{7,6},{8,9},{9,8},{10,11... | collective-permute-start | bytes 393224 | tf_op jit(solution)/shard_map/ppermute | solution.py:22
  46.0 0.7 collective-permute-start.6
  46.7 1.4 collective-permute-start.7
  49.7 4.7 %collective-permute-start.8 = (bf16[32,2048]{1,0:T(8,128)(2,1)S(1)}, bf16[32,2048]{1,0:T(8,128)(2,1)S(1)}, u32[]{:S(2)}, u32[]{:S(2)}) collective-permute-start(bf16[32,2048]{1,0:T(8,128)(2,1)S(1)} %shard_map.42.values_ref), channel_id=1, source_target_pairs={{0,2},{2,0},{1,3},{3,1},{4,6},{6,4},{5,7},{7,5},{8,10},{10,8},{9,1... | collective-permute-start | bytes 393224 | tf_op jit(solution)/shard_map/ppermute | solution.py:22
  55.9 9.1 %collective-permute-start.9 = (bf16[32,2048]{1,0:T(8,128)(2,1)S(1)}, bf16[32,2048]{1,0:T(8,128)(2,1)S(1)}, u32[]{:S(2)}, u32[]{:S(2)}) collective-permute-start(bf16[32,2048]{1,0:T(8,128)(2,1)S(1)} %shard_map.43.values_ref), channel_id=1, source_target_pairs={{0,4},{4,0},{1,5},{5,1},{2,6},{6,2},{3,7},{7,3},{8,12},{12,8},{9,1... | collective-permute-start | bytes 393224 | tf_op jit(solution)/shard_map/ppermute | solution.py:22
  69.0 7.7 %collective-permute-start.10 = (bf16[32,2048]{1,0:T(8,128)(2,1)S(1)}, bf16[32,2048]{1,0:T(8,128)(2,1)S(1)}, u32[]{:S(2)}, u32[]{:S(2)}) collective-permute-start(bf16[32,2048]{1,0:T(8,128)(2,1)S(1)} %shard_map.45), channel_id=1, source_target_pairs={{0,4},{4,0},{1,5},{5,1},{2,6},{6,2},{3,7},{7,3},{8,12},{12,8},{9,1... | collective-permute-start | bytes 393224 | tf_op jit(solution)/shard_map/ppermute | solution.py:22
  76.8 4.6 %collective-permute-start.11 = (bf16[32,2048]{1,0:T(8,128)(2,1)S(1)}, bf16[32,2048]{1,0:T(8,128)(2,1)S(1)}, u32[]{:S(2)}, u32[]{:S(2)}) collective-permute-start(bf16[32,2048]{1,0:T(8,128)(2,1)S(1)} %fusion.14), channel_id=1, source_target_pairs={{0,2},{2,0},{1,3},{3,1},{4,6},{6,4},{5,7},{7,5},{8,10},{10,8},{9,1... | collective-permute-start | bytes 393224 | tf_op jit(solution)/shard_map/ppermute | solution.py:22
  81.5 2.4 %collective-permute-start.12 = (bf16[32,2048]{1,0:T(8,128)(2,1)S(1)}, bf16[32,2048]{1,0:T(8,128)(2,1)S(1)}, u32[]{:S(2)}, u32[]{:S(2)}) collective-permute-start(bf16[32,2048]{1,0:T(8,128)(2,1)S(1)} %fusion.18), channel_id=1, source_target_pairs={{0,1},{1,0},{2,3},{3,2},{4,5},{5,4},{6,7},{7,6},{8,9},{9,8},{10,11... | collective-permute-start | bytes 393224 | tf_op jit(solution)/shard_map/ppermute | solution.py:22
  84.0 0.9 collective-permute-start.13
  84.9 1.4 collective-permute-start.14
  87.8 4.7 %collective-permute-start.15 = (bf16[32,2048]{1,0:T(8,128)(2,1)S(1)}, bf16[32,2048]{1,0:T(8,128)(2,1)S(1)}, u32[]{:S(2)}, u32[]{:S(2)}) collective-permute-start(bf16[32,2048]{1,0:T(8,128)(2,1)S(1)} %shard_map.46.values_ref), channel_id=1, source_target_pairs={{0,2},{2,0},{1,3},{3,1},{4,6},{6,4},{5,7},{7,5},{8,10},{10,8},{9,1... | collective-permute-start | bytes 393224 | tf_op jit(solution)/shard_map/ppermute | solution.py:22
  94.1 9.1 %collective-permute-start.16 = (bf16[32,2048]{1,0:T(8,128)(2,1)S(1)}, bf16[32,2048]{1,0:T(8,128)(2,1)S(1)}, u32[]{:S(2)}, u32[]{:S(2)}) collective-permute-start(bf16[32,2048]{1,0:T(8,128)(2,1)S(1)} %shard_map.47.values_ref), channel_id=1, source_target_pairs={{0,4},{4,0},{1,5},{5,1},{2,6},{6,2},{3,7},{7,3},{8,12},{12,8},{9,1... | collective-permute-start | bytes 393224 | tf_op jit(solution)/shard_map/ppermute | solution.py:22
  107.1 8.7 %collective-permute-start.17 = (bf16[32,2048]{1,0:T(8,128)(2,1)S(1)}, bf16[32,2048]{1,0:T(8,128)(2,1)S(1)}, u32[]{:S(2)}, u32[]{:S(2)}) collective-permute-start(bf16[32,2048]{1,0:T(8,128)(2,1)S(1)} %shard_map.49), channel_id=1, source_target_pairs={{0,4},{4,0},{1,5},{5,1},{2,6},{6,2},{3,7},{7,3},{8,12},{12,8},{9,1... | collective-permute-start | bytes 393224 | tf_op jit(solution)/shard_map/ppermute | solution.py:22
  116.0 4.6 %collective-permute-start.18 = (bf16[32,2048]{1,0:T(8,128)(2,1)S(1)}, bf16[32,2048]{1,0:T(8,128)(2,1)S(1)}, u32[]{:S(2)}, u32[]{:S(2)}) collective-permute-start(bf16[32,2048]{1,0:T(8,128)(2,1)S(1)} %fusion.26), channel_id=1, source_target_pairs={{0,2},{2,0},{1,3},{3,1},{4,6},{6,4},{5,7},{7,5},{8,10},{10,8},{9,1... | collective-permute-start | bytes 393224 | tf_op jit(solution)/shard_map/ppermute | solution.py:22
  120.7 2.4 %collective-permute-start.19 = (bf16[32,2048]{1,0:T(8,128)(2,1)S(1)}, bf16[32,2048]{1,0:T(8,128)(2,1)S(1)}, u32[]{:S(2)}, u32[]{:S(2)}) collective-permute-start(bf16[32,2048]{1,0:T(8,128)(2,1)S(1)} %fusion.30), channel_id=1, source_target_pairs={{0,1},{1,0},{2,3},{3,2},{4,5},{5,4},{6,7},{7,6},{8,9},{9,8},{10,11... | collective-permute-start | bytes 393224 | tf_op jit(solution)/shard_map/ppermute | solution.py:22
  123.1 17.4 %collective-permute-start.20 = (bf16[32,2048]{1,0:T(8,128)(2,1)S(1)}, bf16[32,2048]{1,0:T(8,128)(2,1)S(1)}, u32[]{:S(2)}, u32[]{:S(2)}) collective-permute-start(bf16[32,2048]{1,0:T(8,128)(2,1)S(1)} %fusion.34), channel_id=1, source_target_pairs={{16,24},{17,25},{18,26},{19,27},{20,28},{21,29},{22,30},{23,31}} | collective-permute-start | bytes 393224 | tf_op jit(solution)/shard_map/ppermute | solution.py:26
  140.6 2.0 %collective-permute-start.21 = (bf16[32,2048]{1,0:T(8,128)(2,1)S(1)}, bf16[32,2048]{1,0:T(8,128)(2,1)S(1)}, u32[]{:S(2)}, u32[]{:S(2)}) collective-permute-start(bf16[32,2048]{1,0:T(8,128)(2,1)S(1)} %fusion.50.values_ref), channel_id=1, source_target_pairs={{0,1},{1,0},{2,3},{3,2},{4,5},{5,4},{6,7},{7,6},{8,9},{9,8},{10,11... | collective-permute-start | bytes 393224 | tf_op jit(solution)/shard_map/ppermute | solution.py:22
  144.1 4.7 %collective-permute-start.22 = (bf16[32,2048]{1,0:T(8,128)(2,1)S(1)}, bf16[32,2048]{1,0:T(8,128)(2,1)S(1)}, u32[]{:S(2)}, u32[]{:S(2)}) collective-permute-start(bf16[32,2048]{1,0:T(8,128)(2,1)S(1)} %shard_map.50.values_ref), channel_id=1, source_target_pairs={{0,2},{2,0},{1,3},{3,1},{4,6},{6,4},{5,7},{7,5},{8,10},{10,8},{9,1... | collective-permute-start | bytes 393224 | tf_op jit(solution)/shard_map/ppermute | solution.py:22
  150.3 8.7 %collective-permute-start.23 = (bf16[32,2048]{1,0:T(8,128)(2,1)S(1)}, bf16[32,2048]{1,0:T(8,128)(2,1)S(1)}, u32[]{:S(2)}, u32[]{:S(2)}) collective-permute-start(bf16[32,2048]{1,0:T(8,128)(2,1)S(1)} %shard_map.51.values_ref), channel_id=1, source_target_pairs={{0,4},{4,0},{1,5},{5,1},{2,6},{6,2},{3,7},{7,3},{8,12},{12,8},{9,1... | collective-permute-start | bytes 393224 | tf_op jit(solution)/shard_map/ppermute | solution.py:22
  163.0 8.2 %collective-permute-start.24 = (bf16[32,2048]{1,0:T(8,128)(2,1)S(1)}, bf16[32,2048]{1,0:T(8,128)(2,1)S(1)}, u32[]{:S(2)}, u32[]{:S(2)}) collective-permute-start(bf16[32,2048]{1,0:T(8,128)(2,1)S(1)} %shard_map.53), channel_id=1, source_target_pairs={{0,4},{4,0},{1,5},{5,1},{2,6},{6,2},{3,7},{7,3},{8,12},{12,8},{9,1... | collective-permute-start | bytes 393224 | tf_op jit(solution)/shard_map/ppermute | solution.py:22
  171.2 4.6 %collective-permute-start.25 = (bf16[32,2048]{1,0:T(8,128)(2,1)S(1)}, bf16[32,2048]{1,0:T(8,128)(2,1)S(1)}, u32[]{:S(2)}, u32[]{:S(2)}) collective-permute-start(bf16[32,2048]{1,0:T(8,128)(2,1)S(1)} %fusion.38), channel_id=1, source_target_pairs={{0,2},{2,0},{1,3},{3,1},{4,6},{6,4},{5,7},{7,5},{8,10},{10,8},{9,1... | collective-permute-start | bytes 393224 | tf_op jit(solution)/shard_map/ppermute | solution.py:22
  175.9 5.4 %collective-permute-start.26 = (bf16[32,2048]{1,0:T(8,128)(2,1)S(1)}, bf16[32,2048]{1,0:T(8,128)(2,1)S(1)}, u32[]{:S(2)}, u32[]{:S(2)}) collective-permute-start(bf16[32,2048]{1,0:T(8,128)(2,1)S(1)} %fusion.42), channel_id=1, source_target_pairs={{0,1},{1,0},{2,3},{3,2},{4,5},{5,4},{6,7},{7,6},{8,9},{9,8},{10,11... | collective-permute-start | bytes 393224 | tf_op jit(solution)/shard_map/ppermute | solution.py:22
  177.3 3.4 %copy-start.1 = (bf16[1,1,2048,2048]{3,2,1,0:T(8,128)(2,1)S(1)}, bf16[1,1,2048,2048]{3,2,1,0:T(8,128)(2,1)}, u32[]{:S(2)}) copy-start(bf16[1,1,2048,2048]{3,2,1,0:T(8,128)(2,1)} %param.5) | copy-start | bytes 25165828
